TPU v7x, 32 devices: a whole 2x2x4 slice. The times are simulated.
32 devices in a mesh: dp: 16 (over z, x, core), group: 2 (over y).
Axes of the slice: x: 2, y: 2, z: 4, core: 2. Of those that a mesh axis runs over, the one named last changes fastest.
Arguments:
- inputs: bfloat16 [32768, 2048], P('dp', 'group'), may hold values from -6 to 6
- grad_out: bfloat16 [32768, 2048], P(('dp', 'group')), may hold values from -0.0625 to 0.0625
- weight: bfloat16 [2048, 2048], P('group'), may hold values from -6 to 6
- old_basis: float32 [2048, 256], P('group'), may hold values from -0.125 to 0.125
- first_moment: float32 [256, 2048], P(None, 'dp'), may hold values from -6 to 6
- second_moment: float32 [256, 2048], P(None, 'dp'), may hold values from 0.1 to 3
Outputs:
- new_weight: bfloat16 [2048, 2048], P('group')
- new_first: float32 [256, 2048], P(None, 'dp')
- new_second: float32 [256, 2048], P(None, 'dp')
- new_basis: float32 [2048, 256], P('group')
All inputs are finite; a program needn't handle non-finite values.
Results may differ from a plain program's by a relative error of at most 0.011.
Values may be sent and summed in bfloat16 or wider, within the bound.
No kernel may reach another device: no remote copies, remote signals or barrier semaphores. Data moves between devices by JAX's collectives and lax.ppermute only.
A program may use at most 64 MiB of HBM per device.

v0:
```python
import jax
import jax.numpy as jnp
from jax import lax
from jax.sharding import PartitionSpec as P

NS_STEPS = 5
STEP = 10
BETA_ONE = 0.9
BETA_TWO = 0.99
ADAM_EPS = 1e-08
HIGHEST = lax.Precision.HIGHEST


def matmul(left, right):
    return jnp.dot(left, right, precision=HIGHEST)


def inner_gram(matrix):
    return lax.dot_general(matrix, matrix, (((0,), (0,)), ((), ())), precision=HIGHEST)


def refine_group(subspace):
    squares = lax.psum(jnp.sum(subspace * subspace), "group")
    iterate = subspace / jnp.sqrt(squares)
    for sweep in range(NS_STEPS):
        gram = lax.psum(inner_gram(iterate).astype(jnp.bfloat16), "group").astype(jnp.float32)
        iterate = 1.5 * iterate - 0.5 * matmul(iterate, gram)
    return iterate


def shards(inputs, grad_out, weight, old_basis, first_moment, second_moment):
    partial_grad = lax.dot_general(
        inputs,
        lax.all_gather(grad_out, "group", axis=0, tiled=True),
        (((0,), (0,)), ((), ())),
        preferred_element_type=jnp.float32,
    )
    grad_block = lax.psum_scatter(partial_grad, "dp", scatter_dimension=1, tiled=True)
    projected = lax.psum(matmul(old_basis.T, grad_block).astype(jnp.bfloat16), "group").astype(
        jnp.float32
    )
    new_first = BETA_ONE * first_moment + (1.0 - BETA_ONE) * projected
    new_second = BETA_TWO * second_moment + (1.0 - BETA_TWO) * projected * projected
    direction = (
        new_first
        / (1.0 - BETA_ONE**STEP)
        / (jnp.sqrt(new_second / (1.0 - BETA_TWO**STEP)) + ADAM_EPS)
    )
    col_count = grad_block.shape[1]
    col_offset = lax.axis_index("dp") * col_count
    own_cols = lax.dynamic_slice_in_dim(weight, col_offset, col_count, 1).astype(jnp.float32)
    updated = (own_cols - matmul(old_basis, direction)).astype(jnp.bfloat16)
    new_weight = lax.all_gather(updated, "dp", axis=1, tiled=True)
    subspace_terms = matmul(grad_block, projected.T)
    subspace = lax.psum(subspace_terms, "dp")
    new_basis = refine_group(subspace)
    return (new_weight, new_first, new_second, new_basis)


def solution(mesh):
    return jax.shard_map(
        shards,
        mesh=mesh,
        in_specs=(
            P("dp", "group"),
            P(("dp", "group"), None),
            P("group", None),
            P("group", None),
            P(None, "dp"),
            P(None, "dp"),
        ),
        out_specs=(P("group", None), P(None, "dp"), P(None, "dp"), P("group", None)),
        check_vma=False,
    )
```

profile of v0, /device:TPU:0, one launch (start us, length us, event | category | flops | bytes accessed | tf_op | source)
XLA Modules:
  0.0 558.3 jit_solution(406713574473706663)
XLA Ops:
  8.0 108.3 %all-gather.3.cloned.1.call-done = bf16[2048,2048]{1,0:T(8,128)(2,1)} async-done(((bf16[1024,2048]{1,0:T(8,128)(2,1)}), bf16[2048,2048]{1,0:T(8,128)(2,1)}) %all-gather.3.cloned.1.call-update) | async-done | bytes 8388624 | tf_op jit(solution)/shard_map/all_gather | solution.py:34
  116.3 14.6 %fusion.21 = f32[1024,2048]{1,0:T(8,128)} fusion(bf16[2048,1024]{1,0:T(8,128)(2,1)} %param.6, bf16[2048,2048]{1,0:T(8,128)(2,1)} %all-gather.3.cloned.1.call-done), kind=kOutput, calls=%fused_computation.38 | convolution fusion | flops 8589934592 | bytes 20971520 | tf_op jit(solution)/shard_map/dot_general | solution.py:32
  130.9 103.7 %reduce-scatter.2.cloned.1.call-done = f32[1024,128]{1,0:T(8,128)} async-done(((f32[1024,2048]{1,0:T(8,128)}), f32[1024,128]{1,0:T(8,128)}) %reduce-scatter.2.cloned.1.call-update) | async-done | bytes 524304 | tf_op jit(solution)/shard_map/reduce_scatter | solution.py:38
  234.6 2.7 fusion.7
  237.4 20.7 %all-reduce.8.cloned.1.call-done = bf16[256,128]{0,1:T(8,128)(2,1)} async-done(((bf16[256,128]{0,1:T(8,128)(2,1)}), bf16[256,128]{0,1:T(8,128)(2,1)}) %all-reduce.8.cloned.1.call-update) | async-done | bytes 65552 | tf_op jit(solution)/shard_map/psum | solution.py:39
  258.1 2.6 fusion.22
  260.8 95.1 %all-reduce.10.cloned.1.call-done = f32[1024,256]{1,0:T(8,128)} async-done(((f32[1024,256]{1,0:T(8,128)}), f32[1024,256]{1,0:T(8,128)}) %all-reduce.10.cloned.1.call-update) | async-done | bytes 1048592 | tf_op jit(solution)/shard_map/psum | solution.py:55
  355.8 2.2 multiply_reduce_fusion
  358.0 5.5 psum.58
  364.3 4.0 convolution_convert_fusion.4
  368.4 20.7 %all-reduce.12.cloned.1.call-done = bf16[256,256]{1,0:T(8,128)(2,1)} async-done(((bf16[256,256]{1,0:T(8,128)(2,1)}), bf16[256,256]{1,0:T(8,128)(2,1)}) %all-reduce.12.cloned.1.call-update) | async-done | bytes 131088 | tf_op jit(solution)/shard_map/psum | solution.py:26
  389.1 1.6 fusion.4
  390.7 2.5 convolution_convert_fusion.3
  393.5 21.4 %all-reduce.14.cloned.1.call-done = bf16[256,256]{1,0:T(8,128)(2,1)} async-done(((bf16[256,256]{1,0:T(8,128)(2,1)}), bf16[256,256]{1,0:T(8,128)(2,1)}) %all-reduce.14.cloned.1.call-update) | async-done | bytes 131088 | tf_op jit(solution)/shard_map/psum | solution.py:26
  414.9 1.5 fusion.3
  416.4 2.5 convolution_convert_fusion.2
  419.0 1.0 constant_dynamic-slice_fusion
  420.0 0.9 copy.16
  421.0 0.8 copy.12
  421.7 18.9 %all-reduce.16.cloned.1.call-done = bf16[256,256]{1,0:T(8,128)(2,1)} async-done(((bf16[256,256]{1,0:T(8,128)(2,1)}), bf16[256,256]{1,0:T(8,128)(2,1)}) %all-reduce.16.cloned.1.call-update) | async-done | bytes 131088 | tf_op jit(solution)/shard_map/psum | solution.py:26
  440.6 1.5 fusion.2
  442.2 2.5 convolution_convert_fusion.1
  444.7 1.0 fusion.8
  445.7 20.6 %all-reduce.18.cloned.1.call-done = bf16[256,256]{1,0:T(8,128)(2,1)} async-done(((bf16[256,256]{1,0:T(8,128)(2,1)}), bf16[256,256]{1,0:T(8,128)(2,1)}) %all-reduce.18.cloned.1.call-update) | async-done | bytes 131088 | tf_op jit(solution)/shard_map/psum | solution.py:26
  466.4 1.5 fusion.1
  467.9 2.5 convolution_convert_fusion
  470.5 2.9 fusion.6
  473.4 0.8 copy.14
  474.9 17.2 %all-reduce.20.cloned.1.call-done = bf16[256,256]{1,0:T(8,128)(2,1)} async-done(((bf16[256,256]{1,0:T(8,128)(2,1)}), bf16[256,256]{1,0:T(8,128)(2,1)}) %all-reduce.20.cloned.1.call-update) | async-done | bytes 131088 | tf_op jit(solution)/shard_map/psum | solution.py:26
  492.1 2.5 fusion
  494.6 50.5 %all-gather.5.cloned.1.call-done = bf16[1024,2048]{0,1:T(8,128)(2,1)} async-done(((bf16[1024,128]{0,1:T(8,128)(2,1)}), bf16[1024,2048]{0,1:T(8,128)(2,1)}) %all-gather.5.cloned.1.call-update) | async-done | bytes 4194320 | tf_op jit(solution)/shard_map/all_gather | solution.py:53
  545.1 6.4 %copy.13 = bf16[1024,2048]{1,0:T(8,128)(2,1)} copy(bf16[1024,2048]{0,1:T(8,128)(2,1)} %all-gather.5.cloned.1.call-done) | data formatting | bytes 8388608
  (30 shorter events, 2.3 us)
Async XLA Ops:
  7.2 227.5 %copy-start = (f32[1024,256]{1,0:T(8,128)S(1)}, f32[1024,256]{1,0:T(8,128)}, u32[]{:S(2)}) copy-start(f32[1024,256]{1,0:T(8,128)} %param.9) | copy-start | bytes 3145732
  7.2 109.1 %all-gather.3.cloned.1.call-start = ((), (), s32[]{:S(2)}) async-start(), calls=%async_computation.1 | async-start | bytes 12582912 | tf_op jit(solution)/shard_map/all_gather | solution.py:34
  7.9 226.7 %reduce-scatter.2.cloned.1.call-start = ((), (), s32[]{:S(2)}) async-start(), calls=%async_computation.2 | async-start | bytes 8912896 | tf_op jit(solution)/shard_map/reduce_scatter | solution.py:38
  130.9 127.2 %all-reduce.8.cloned.1.call-start = ((), (), s32[]{:S(2)}) async-start(), calls=%async_computation.3 | async-start | bytes 131072 | tf_op jit(solution)/shard_map/psum | solution.py:39
  237.4 118.5 %all-reduce.10.cloned.1.call-start = ((), (), s32[]{:S(2)}) async-start(), calls=%async_computation.5 | async-start | bytes 2097152 | tf_op jit(solution)/shard_map/psum | solution.py:55
  260.7 128.4 %all-reduce.12.cloned.1.call-start = ((), (), s32[]{:S(2)}) async-start(), calls=%async_computation.6 | async-start | bytes 262144 | tf_op jit(solution)/shard_map/psum | solution.py:26
  355.8 33.3 %copy-start.1 = (f32[1024,256]{1,0:T(8,128)S(1)}, f32[1024,256]{1,0:T(8,128)}, u32[]{:S(2)}) copy-start(f32[1024,256]{1,0:T(8,128)} %all-reduce.10.cloned.1.call-done) | copy-start | bytes 3145732
  368.3 46.6 %all-reduce.14.cloned.1.call-start = ((), (), s32[]{:S(2)}) async-start(), calls=%async_computation.7 | async-start | bytes 262144 | tf_op jit(solution)/shard_map/psum | solution.py:26
  390.7 30.2 %copy-start.2 = (f32[256,128]{1,0:T(8,128)S(1)}, f32[256,128]{1,0:T(8,128)}, u32[]{:S(2)}) copy-start(f32[256,128]{1,0:T(8,128)} %param.10) | copy-start | bytes 393220
  390.7 30.3 %copy-start.3 = (f32[256,128]{1,0:T(8,128)S(1)}, f32[256,128]{1,0:T(8,128)}, u32[]{:S(2)}) copy-start(f32[256,128]{1,0:T(8,128)} %param.11) | copy-start | bytes 393220
  393.2 47.4 %all-reduce.16.cloned.1.call-start = ((), (), s32[]{:S(2)}) async-start(), calls=%async_computation.8 | async-start | bytes 262144 | tf_op jit(solution)/shard_map/psum | solution.py:26
  419.0 47.4 %all-reduce.18.cloned.1.call-start = ((), (), s32[]{:S(2)}) async-start(), calls=%async_computation.9 | async-start | bytes 262144 | tf_op jit(solution)/shard_map/psum | solution.py:26
  444.7 47.4 %all-reduce.20.cloned.1.call-start = ((), (), s32[]{:S(2)}) async-start(), calls=%async_computation.10 | async-start | bytes 262144 | tf_op jit(solution)/shard_map/psum | solution.py:26
  470.4 74.7 %all-gather.5.cloned.1.call-start = ((), (), s32[]{:S(2)}) async-start(), calls=%async_computation.4 | async-start | bytes 4456448 | tf_op jit(solution)/shard_map/all_gather | solution.py:53
Sparse Core Ops, SparseCore 0:
  9.5 106.6 all-gather.2
  131.0 103.5 reduce-scatter.1
  237.5 20.5 all-reduce.7
  262.0 93.7 all-reduce.9
  368.4 20.6 all-reduce.11
  393.4 21.5 all-reduce.13
  419.1 21.5 all-reduce.15
  444.8 21.5 all-reduce.17
  470.5 21.5 all-reduce.19
  494.7 50.3 all-gather.4
where the time goes:
time: 559 us; the launch traced here: 558 us
  waiting for transfers between devices  478 us (86%)
  matrix products  45.4 us (8%)
  between operations  15 us (3%)
  local copies, waits for them, and re-layouts  10.6 us (2%)
    all_gather x1, waiting for transfers between devices, shards(): lax.all_gather(grad_out, 'group', axis=0, tiled=True)  108 us
    reduce_scatter x1, waiting for transfers between devices, shards(): lax.psum_scatter(partial_grad, 'dp', scatter_dimension=1, tiled=True)  104 us
    psum x5, waiting for transfers between devices, refine_group(): lax.psum(inner_gram(iterate).astype(jnp.bfloat16), 'group')  99 us
    psum x1, waiting for transfers between devices, shards(): subspace = lax.psum(subspace_terms, 'dp')  95.1 us
    all_gather x1, waiting for transfers between devices, shards(): new_weight = lax.all_gather(updated, 'dp', axis=1, tiled=True)  50.5 us
    psum x1, waiting for transfers between devices, shards(): lax.psum(matmul(old_basis.T, grad_block).astype(jnp.bfloat16), 'group')  20.7 us
    dot_general x8, matrix products, matmul(): return jnp.dot(left, right, precision=HIGHEST)  16.8 us
    dot_general x1, matrix products, shards(): lax.dot_general(inputs, lax.all_gather(grad_out, 'group', axis=0, tiled=T...  14.6 us
  transfers between devices with their start and end apart: 10, of which 10 were waited for; matrix products, arithmetic and copies ran while one was open for 2% of the time, Pallas kernels for 0%

commit v1 on v0

--- a/solution.py
+++ b/solution.py
@@ -50,7 +50,9 @@
     col_offset = lax.axis_index("dp") * col_count
     own_cols = lax.dynamic_slice_in_dim(weight, col_offset, col_count, 1).astype(jnp.float32)
     updated = (own_cols - matmul(old_basis, direction)).astype(jnp.bfloat16)
-    new_weight = lax.all_gather(updated, "dp", axis=1, tiled=True)
+    new_weight = jnp.concatenate(
+        lax.all_to_all(jnp.stack([updated] * lax.axis_size("dp")), "dp", 0, 0), axis=1
+    )
     subspace_terms = matmul(grad_block, projected.T)
     subspace = lax.psum(subspace_terms, "dp")
     new_basis = refine_group(subspace)

time: 559 us -> 585 us (1.047)
  waiting for transfers between devices: 478 us -> 493 us
  local copies, waits for them, and re-layouts: 10.6 us -> 18.7 us
    psum x1, waiting for transfers between devices: 95.1 us -> 155 us  [shards(): subspace = lax.psum(subspace_terms, 'dp')]
    all_gather x1 -> x0, waiting for transfers between devices: 50.5 us -> none  [shards(): new_weight = lax.all_gather(updated, 'dp', axis=1, tiled=True)]
    psum x5, waiting for transfers between devices: 99 us -> 106 us  [refine_group(): lax.psum(inner_gram(iterate).astype(jnp.bfloat16), 'group')]
    all_to_all x0 -> x1, local copies, waits for them, and re-layouts: none -> 6.44 us  [shards(): lax.all_to_all(jnp.stack([updated] * lax.axis_size('dp')), 'dp', 0, 0)]
  transfers between devices with their start and end apart: 10 -> 10, of which waited for: 10 -> 9; matrix products, arithmetic and copies ran while one was open for 2% -> 5% of each run, Pallas kernels for 0% -> 0%
where the time goes in v1:
time: 585 us; the launch traced here: 584 us
  waiting for transfers between devices  493 us (84%)
  matrix products  42.8 us (7%)
  local copies, waits for them, and re-layouts  18.7 us (3%)
  between operations  14.7 us (3%)
  starting transfers between devices  6.35 us (1%)
    psum x1, waiting for transfers between devices, shards(): subspace = lax.psum(subspace_terms, 'dp')  155 us
    all_gather x1, waiting for transfers between devices, shards(): lax.all_gather(grad_out, 'group', axis=0, tiled=True)  108 us
    psum x5, waiting for transfers between devices, refine_group(): lax.psum(inner_gram(iterate).astype(jnp.bfloat16), 'group')  106 us
    reduce_scatter x1, waiting for transfers between devices, shards(): lax.psum_scatter(partial_grad, 'dp', scatter_dimension=1, tiled=True)  104 us
    psum x1, waiting for transfers between devices, shards(): lax.psum(matmul(old_basis.T, grad_block).astype(jnp.bfloat16), 'group')  19.4 us
    dot_general x1, matrix products, shards(): lax.dot_general(inputs, lax.all_gather(grad_out, 'group', axis=0, tiled=T...  14.7 us
    dot_general x8, matrix products, matmul(): return jnp.dot(left, right, precision=HIGHEST)  14.1 us
    dot_general x5, matrix products, inner_gram(): lax.dot_general(matrix, matrix, (((0,), (0,)), ((), ())), precision=HIGHEST)  14 us
  transfers between devices with their start and end apart: 10, of which 9 were waited for; matrix products, arithmetic and copies ran while one was open for 5% of the time, Pallas kernels for 0%

profile of v1, /device:TPU:0, one launch (start us, length us, event | category | flops | bytes accessed | tf_op | source)
XLA Modules:
  0.0 583.9 jit_solution(16170019780828477489)
XLA Ops:
  8.0 108.3 %all-gather.2.cloned.1.call-done = bf16[2048,2048]{1,0:T(8,128)(2,1)} async-done(((bf16[1024,2048]{1,0:T(8,128)(2,1)}), bf16[2048,2048]{1,0:T(8,128)(2,1)}) %all-gather.2.cloned.1.call-update) | async-done | bytes 8388624 | tf_op jit(solution)/shard_map/all_gather | solution.py:34
  116.3 14.7 %fusion.21 = f32[1024,2048]{1,0:T(8,128)} fusion(bf16[2048,1024]{1,0:T(8,128)(2,1)} %param.6, bf16[2048,2048]{1,0:T(8,128)(2,1)} %all-gather.2.cloned.1.call-done), kind=kOutput, calls=%fused_computation.38 | convolution fusion | flops 8589934592 | bytes 20971520 | tf_op jit(solution)/shard_map/dot_general | solution.py:32
  131.1 103.7 %reduce-scatter.2.cloned.1.call-done = f32[1024,128]{1,0:T(8,128)} async-done(((f32[1024,2048]{1,0:T(8,128)}), f32[1024,128]{1,0:T(8,128)}) %reduce-scatter.2.cloned.1.call-update) | async-done | bytes 524304 | tf_op jit(solution)/shard_map/reduce_scatter | solution.py:38
  234.8 2.7 fusion.7
  237.5 1.0 constant_dynamic-slice_fusion
  238.9 19.4 %all-reduce.8.cloned.1.call-done = bf16[256,128]{0,1:T(8,128)(2,1)} async-done(((bf16[256,128]{0,1:T(8,128)(2,1)}), bf16[256,128]{0,1:T(8,128)(2,1)}) %all-reduce.8.cloned.1.call-update) | async-done | bytes 65552 | tf_op jit(solution)/shard_map/psum | solution.py:39
  258.2 0.9 fusion.8
  259.1 1.2 fusion.6
  260.5 2.8 stack.2
  263.3 5.8 all-to-all-start
  269.2 1.5 fusion.22
  270.8 155.0 %all-reduce.10.cloned.1.call-done = f32[1024,256]{1,0:T(8,128)} async-done(((f32[1024,256]{1,0:T(8,128)}), f32[1024,256]{1,0:T(8,128)}) %all-reduce.10.cloned.1.call-update) | async-done | bytes 1048592 | tf_op jit(solution)/shard_map/psum | solution.py:57
  425.8 2.2 multiply_reduce_fusion
  428.0 5.5 psum.58
  434.2 4.0 convolution_convert_fusion.4
  438.5 20.6 %all-reduce.12.cloned.1.call-done = bf16[256,256]{1,0:T(8,128)(2,1)} async-done(((bf16[256,256]{1,0:T(8,128)(2,1)}), bf16[256,256]{1,0:T(8,128)(2,1)}) %all-reduce.12.cloned.1.call-update) | async-done | bytes 131088 | tf_op jit(solution)/shard_map/psum | solution.py:26
  459.1 1.6 fusion.4
  460.7 2.5 convolution_convert_fusion.3
  463.2 21.6 %all-reduce.14.cloned.1.call-done = bf16[256,256]{1,0:T(8,128)(2,1)} async-done(((bf16[256,256]{1,0:T(8,128)(2,1)}), bf16[256,256]{1,0:T(8,128)(2,1)}) %all-reduce.14.cloned.1.call-update) | async-done | bytes 131088 | tf_op jit(solution)/shard_map/psum | solution.py:26
  484.9 1.5 fusion.3
  486.4 2.5 convolution_convert_fusion.2
  489.0 21.6 %all-reduce.16.cloned.1.call-done = bf16[256,256]{1,0:T(8,128)(2,1)} async-done(((bf16[256,256]{1,0:T(8,128)(2,1)}), bf16[256,256]{1,0:T(8,128)(2,1)}) %all-reduce.16.cloned.1.call-update) | async-done | bytes 131088 | tf_op jit(solution)/shard_map/psum | solution.py:26
  510.6 1.5 fusion.2
  512.1 2.5 convolution_convert_fusion.1
  514.7 21.6 %all-reduce.18.cloned.1.call-done = bf16[256,256]{1,0:T(8,128)(2,1)} async-done(((bf16[256,256]{1,0:T(8,128)(2,1)}), bf16[256,256]{1,0:T(8,128)(2,1)}) %all-reduce.18.cloned.1.call-update) | async-done | bytes 131088 | tf_op jit(solution)/shard_map/psum | solution.py:26
  536.3 1.5 fusion.1
  537.8 2.5 convolution_convert_fusion
  540.4 0.8 copy.28
  541.9 20.2 %all-reduce.20.cloned.1.call-done = bf16[256,256]{1,0:T(8,128)(2,1)} async-done(((bf16[256,256]{1,0:T(8,128)(2,1)}), bf16[256,256]{1,0:T(8,128)(2,1)}) %all-reduce.20.cloned.1.call-update) | async-done | bytes 131088 | tf_op jit(solution)/shard_map/psum | solution.py:26
  562.0 2.5 fusion
  564.5 6.4 %copy.26 = bf16[16,1024,128]{1,2,0:T(8,128)(2,1)} copy(bf16[16,1024,128]{2,1,0:T(8,128)(2,1)} %all-to-all-done) | data formatting | bytes 8388608 | tf_op jit(solution)/shard_map/all_to_all | solution.py:54
  571.0 6.4 %copy.27 = bf16[1024,2048]{1,0:T(8,128)(2,1)} copy(bf16[1024,2048]{0,1:T(8,128)(2,1)} %bitcast.35) | data formatting | bytes 8388608
  (36 shorter events, 2.6 us)
Async XLA Ops:
  7.2 227.6 %copy-start = (f32[1024,256]{1,0:T(8,128)S(1)}, f32[1024,256]{1,0:T(8,128)}, u32[]{:S(2)}) copy-start(f32[1024,256]{1,0:T(8,128)} %param.9) | copy-start | bytes 3145732
  7.2 109.1 %all-gather.2.cloned.1.call-start = ((), (), s32[]{:S(2)}) async-start(), calls=%async_computation.2 | async-start | bytes 12582912 | tf_op jit(solution)/shard_map/all_gather | solution.py:34
  7.9 226.9 %reduce-scatter.2.cloned.1.call-start = ((), (), s32[]{:S(2)}) async-start(), calls=%async_computation.3 | async-start | bytes 8912896 | tf_op jit(solution)/shard_map/reduce_scatter | solution.py:38
  131.0 107.6 %copy-start.4 = (f32[256,128]{1,0:T(8,128)S(1)}, f32[256,128]{1,0:T(8,128)}, u32[]{:S(2)}) copy-start(f32[256,128]{1,0:T(8,128)} %param.10) | copy-start | bytes 393220
  131.0 107.8 %copy-start.5 = (f32[256,128]{1,0:T(8,128)S(1)}, f32[256,128]{1,0:T(8,128)}, u32[]{:S(2)}) copy-start(f32[256,128]{1,0:T(8,128)} %param.11) | copy-start | bytes 393220
  131.0 127.2 %all-reduce.8.cloned.1.call-start = ((), (), s32[]{:S(2)}) async-start(), calls=%async_computation.4 | async-start | bytes 131072 | tf_op jit(solution)/shard_map/psum | solution.py:39
  263.3 5.9 %copy-start.1 = (f32[1024,128]{1,0:T(8,128)S(1)}, f32[1024,128]{1,0:T(8,128)}, u32[]{:S(2)}) copy-start(f32[1024,128]{1,0:T(8,128)} %reduce-scatter.2.cloned.1.call-done) | copy-start | bytes 1572868
  263.3 5.9 %copy-start.3 = (bf16[256,128]{0,1:T(8,128)(2,1)S(1)}, bf16[256,128]{0,1:T(8,128)(2,1)}, u32[]{:S(2)}) copy-start(bf16[256,128]{0,1:T(8,128)(2,1)} %all-reduce.8.cloned.1.call-done) | copy-start | bytes 196612
  263.3 301.2 %all-to-all-start = ((bf16[16,1024,128]{2,1,0:T(8,128)(2,1)}), bf16[16,1024,128]{2,1,0:T(8,128)(2,1)}, u32[]{:S(2)}, u32[]{:S(2)}) async-start(bf16[16,1024,128]{2,1,0:T(8,128)(2,1)} %stack.2), calls=%async_computation.1 | async-start | bytes 8388608 | tf_op jit(solution)/shard_map/all_to_all | solution.py:54
  269.2 156.7 %all-reduce.10.cloned.1.call-start = ((), (), s32[]{:S(2)}) async-start(), calls=%async_computation.5 | async-start | bytes 2097152 | tf_op jit(solution)/shard_map/psum | solution.py:57
  270.8 188.3 %all-reduce.12.cloned.1.call-start = ((), (), s32[]{:S(2)}) async-start(), calls=%async_computation.6 | async-start | bytes 262144 | tf_op jit(solution)/shard_map/psum | solution.py:26
  425.8 33.3 %copy-start.2 = (f32[1024,256]{1,0:T(8,128)S(1)}, f32[1024,256]{1,0:T(8,128)}, u32[]{:S(2)}) copy-start(f32[1024,256]{1,0:T(8,128)} %all-reduce.10.cloned.1.call-done) | copy-start | bytes 3145732
  438.3 46.6 %all-reduce.14.cloned.1.call-start = ((), (), s32[]{:S(2)}) async-start(), calls=%async_computation.7 | async-start | bytes 262144 | tf_op jit(solution)/shard_map/psum | solution.py:26
  463.2 47.4 %all-reduce.16.cloned.1.call-start = ((), (), s32[]{:S(2)}) async-start(), calls=%async_computation.8 | async-start | bytes 262144 | tf_op jit(solution)/shard_map/psum | solution.py:26
  488.9 47.4 %all-reduce.18.cloned.1.call-start = ((), (), s32[]{:S(2)}) async-start(), calls=%async_computation.9 | async-start | bytes 262144 | tf_op jit(solution)/shard_map/psum | solution.py:26
  514.6 47.4 %all-reduce.20.cloned.1.call-start = ((), (), s32[]{:S(2)}) async-start(), calls=%async_computation.10 | async-start | bytes 262144 | tf_op jit(solution)/shard_map/psum | solution.py:26
Sparse Core Ops, SparseCore 0:
  9.5 106.6 all-gather.1
  131.1 103.5 reduce-scatter.1
  237.6 20.5 all-reduce.7
  273.7 152.0 all-reduce.9
  438.4 20.6 all-reduce.11
  463.3 21.5 all-reduce.13
  489.0 21.5 all-reduce.15
  514.8 21.5 all-reduce.17
  540.5 21.5 all-reduce.19
